TPU v7x, 256 devices: a whole 4x4x8 slice. The times are simulated.
256 devices in a mesh: rep: 16 (over z, core), exp: 16 (over y, x).
Axes of the slice: x: 4, y: 4, z: 8, core: 2. Of those that a mesh axis runs over, the one named last changes fastest.
Arguments:
- tokens: bfloat16 [2048, 2048], P('exp'), may hold values from -6 to 6
- expert_ids: int32 [2048, 2], P('exp'), may hold values from 0 to 15, all different within a row; in each aligned block of 128 rows (0 to 127, 128 to 255, ...) at most 32 rows name the same one
- gate_values: float32 [2048, 2], P('exp'), may hold values from 0.2 to 1
- grad_out: bfloat16 [2048, 2048], P('exp'), may hold values from -6 to 6
- w_up: bfloat16 [16, 2048, 8192], P('exp', None, 'rep'), may hold values from -0.125 to 0.125
- w_down: bfloat16 [16, 8192, 2048], P('exp', 'rep'), may hold values from -0.0625 to 0.0625
Outputs:
- mixed: bfloat16 [2048, 2048], P('exp', 'rep')
- grad_tokens: bfloat16 [2048, 2048], P('exp', 'rep')
- grad_w_up: bfloat16 [16, 2048, 8192], P('exp', None, 'rep')
- grad_w_down: bfloat16 [16, 8192, 2048], P('exp', 'rep')
Inputs may be any that keep to these rules, and one draw needn't show every extreme that they name: `expert_ids`: each row names 2 different experts. Within the rows of one index of exp (aligned blocks of 128 rows) no expert is named by more than 32 rows, a bound that some block reaches.
All inputs are finite; a program needn't handle non-finite values.
Results may differ from a plain program's by a relative error of at most 0.022.
Values may be sent and summed in bfloat16 or wider, within the bound.
No kernel may reach another device: no remote copies, remote signals or barrier semaphores. Data moves between devices by JAX's collectives and lax.ppermute only.
A program may use at most 128 MiB of HBM per device.

v0:
```python
import jax
import jax.numpy as jnp
from jax import lax
from jax.sharding import PartitionSpec as P


def plan_slots(routed, experts, capacity):
    flat_ids = routed.reshape(-1)
    onehot = (flat_ids[:, None] == jnp.arange(experts, dtype=jnp.int32)[None, :]).astype(jnp.int32)
    before = jnp.cumsum(onehot, axis=0) - onehot
    position = jnp.sum(before * onehot, axis=1)
    counts = jnp.sum(onehot, axis=0)
    slotting_labels = flat_ids * capacity + position
    placed = (
        slotting_labels[None, :] == jnp.arange(experts * capacity, dtype=jnp.int32)[:, None]
    ).astype(jnp.bfloat16)
    return (placed, counts)


def expert_math(rows_in, rows_grad, live_mask, up_weight, down_weight):
    preact = jnp.dot(rows_in, up_weight, preferred_element_type=jnp.float32)
    sigmoid_val = jax.nn.sigmoid(preact)
    keep = live_mask[:, None]
    hidden_units = jnp.where(keep, preact * sigmoid_val, 0.0).astype(jnp.bfloat16)
    out_part = jnp.dot(hidden_units, down_weight, preferred_element_type=jnp.float32)
    grad_hidden = lax.dot_general(
        rows_grad, down_weight, (((1,), (1,)), ((), ())), preferred_element_type=jnp.float32
    )
    slope = sigmoid_val * (1.0 + preact * (1.0 - sigmoid_val))
    gradient_before_activation = jnp.where(keep, grad_hidden * slope, 0.0).astype(jnp.bfloat16)
    grad_down_e = lax.dot_general(
        hidden_units, rows_grad, (((0,), (0,)), ((), ())), preferred_element_type=jnp.float32
    )
    grad_up_e = lax.dot_general(
        rows_in,
        gradient_before_activation,
        (((0,), (0,)), ((), ())),
        preferred_element_type=jnp.float32,
    )
    dx_part = lax.dot_general(
        gradient_before_activation,
        up_weight,
        (((1,), (1,)), ((), ())),
        preferred_element_type=jnp.float32,
    )
    return (out_part, dx_part, grad_up_e, grad_down_e)


def local(tokens, expert_ids, gate_values, grad_out, w_up, w_down):
    n_rep = lax.axis_size("rep")
    n_exp = lax.axis_size("exp")
    tok_count, width = tokens.shape
    top_k = expert_ids.shape[1]
    pair_count = tok_count * top_k
    capacity = max(2, min(tok_count, 2 * tok_count * top_k // n_exp))
    cols = width // n_rep
    up_weight = w_up[0]
    down_weight = w_down[0]
    grad_rows = (gate_values[:, :, None] * grad_out[:, None, :].astype(jnp.float32)).astype(
        jnp.bfloat16
    )
    grad_rows = grad_rows.reshape(pair_count, width)
    placed, counts = plan_slots(expert_ids, n_exp, capacity)
    summed = placed.reshape(n_exp * capacity, tok_count, top_k).sum(axis=2)
    sent_in = jnp.dot(summed, tokens, preferred_element_type=jnp.float32).astype(jnp.bfloat16)
    sent_grad = jnp.dot(placed, grad_rows, preferred_element_type=jnp.float32).astype(jnp.bfloat16)
    count_parts = jnp.stack([counts // 16, counts % 16], axis=1).astype(jnp.bfloat16)
    got_in, got_grad, got_counts = (
        lax.all_to_all(
            sent_in.reshape(n_exp, capacity, width), "exp", split_axis=0, concat_axis=0, tiled=True
        ),
        lax.all_to_all(
            sent_grad.reshape(n_exp, capacity, width),
            "exp",
            split_axis=0,
            concat_axis=0,
            tiled=True,
        ),
        lax.all_to_all(count_parts, "exp", split_axis=0, concat_axis=0, tiled=True),
    )
    count_values = got_counts[:, 0].astype(jnp.float32) * 16.0 + got_counts[:, 1].astype(
        jnp.float32
    )
    slot_mask = jnp.arange(capacity, dtype=jnp.float32)[None, :] < count_values[:, None]
    rows_in = got_in.reshape(-1, width)
    rows_grad = got_grad.reshape(-1, width)
    live_mask = slot_mask.reshape(-1)
    out_part, dx_part, grad_up_e, grad_down_e = expert_math(
        rows_in, rows_grad, live_mask, up_weight, down_weight
    )
    total_out, total_dx = (
        lax.psum(out_part.astype(jnp.bfloat16), "rep").astype(jnp.float32),
        lax.psum(dx_part.astype(jnp.bfloat16), "rep").astype(jnp.float32),
    )
    col_start = lax.axis_index("rep") * cols
    summed_out = lax.dynamic_slice_in_dim(total_out, col_start, cols, 1)
    summed_dx = lax.dynamic_slice_in_dim(total_dx, col_start, cols, 1)
    back_out, back_dx = (
        lax.all_to_all(
            summed_out.astype(jnp.bfloat16).reshape(n_exp, capacity, cols),
            "exp",
            split_axis=0,
            concat_axis=0,
            tiled=True,
        ),
        lax.all_to_all(
            summed_dx.astype(jnp.bfloat16).reshape(n_exp, capacity, cols),
            "exp",
            split_axis=0,
            concat_axis=0,
            tiled=True,
        ),
    )
    pair_out = jnp.einsum(
        "st,sd->td",
        placed,
        back_out.reshape(n_exp * capacity, cols),
        preferred_element_type=jnp.float32,
    )
    pair_dx = jnp.einsum(
        "st,sd->td",
        placed,
        back_dx.reshape(n_exp * capacity, cols),
        preferred_element_type=jnp.float32,
    )
    mixed = jnp.sum(gate_values[:, :, None] * pair_out.reshape(tok_count, top_k, cols), axis=1)
    grad_tokens = jnp.sum(pair_dx.reshape(tok_count, top_k, cols), axis=1)
    return (
        mixed.astype(jnp.bfloat16),
        grad_tokens.astype(jnp.bfloat16),
        grad_up_e.astype(jnp.bfloat16)[None],
        grad_down_e.astype(jnp.bfloat16)[None],
    )


def solution(mesh):
    return jax.shard_map(
        local,
        mesh=mesh,
        in_specs=(
            P("exp", None),
            P("exp", None),
            P("exp", None),
            P("exp", None),
            P("exp", None, "rep"),
            P("exp", "rep", None),
        ),
        out_specs=(P("exp", "rep"), P("exp", "rep"), P("exp", None, "rep"), P("exp", "rep", None)),
        check_vma=False,
    )
```

profile of v0, /device:TPU:2, one launch (start us, length us, event | category | flops | bytes accessed | tf_op | source)
XLA Modules:
  0.0 255.9 jit_solution(6075189790972760029)
XLA Ops:
  7.2 0.9 copy.37
  8.4 0.6 reduce-window.6
  9.0 0.2 slice_reduce_fusion
  9.2 0.1 convert_reduce_fusion
  9.4 0.7 copy.41
  10.1 7.5 %all-to-all-start = ((bf16[16,1,2]{2,1,0:T(2,128)(2,1)}), bf16[16,1,2]{2,1,0:T(2,128)(2,1)S(1)}, u32[]{:S(2)}, u32[]{:S(2)}) async-start(bf16[16,1,2]{2,1,0:T(2,128)(2,1)} %copy.41), calls=%async_computation | async-start | bytes 16384 | tf_op jit(solution)/shard_map/all_to_all | solution.py:79
  17.8 0.7 multiply_add_fusion.1
  18.6 3.1 %convolution_convert_fusion.1 = bf16[512,2048]{1,0:T(8,128)(2,1)} fusion(bf16[512,128]{1,0:T(8,128)(2,1)S(1)} %fusion.23, bf16[128,2048]{1,0:T(8,128)(2,1)} %param.6), kind=kOutput, calls=%fused_computation.1 | convolution fusion | flops 269484032 | bytes 2752512 | tf_op jit(solution)/shard_map/dot_general | solution.py:65
  21.6 2.1 all-to-all-done
  23.7 5.7 %all-to-all-start.1 = ((bf16[16,32,2048]{2,1,0:T(8,128)(2,1)}), bf16[16,32,2048]{2,1,0:T(8,128)(2,1)}, u32[]{:S(2)}, u32[]{:S(2)}) async-start(bf16[16,32,2048]{2,1,0:T(8,128)(2,1)} %bitcast.82), calls=%async_computation.1 | async-start | bytes 4194304 | tf_op jit(solution)/shard_map/all_to_all | solution.py:69
  29.8 2.4 mul.76
  32.1 3.7 %mul.77 = f32[256,2048]{1,0:T(8,128)} reshape(f32[128,2,2048]{2,1,0:T(2,128)} %mul.76) | data formatting | bytes 4194304 | tf_op jit(solution)/shard_map/mul | solution.py:59
  35.8 3.7 %convolution_convert_fusion = bf16[512,2048]{1,0:T(8,128)(2,1)} fusion(f32[256,2048]{1,0:T(8,128)} %mul.77, f32[256]{0:T(256)S(1)} %mul.74, s32[256]{0:T(256)S(1)} %multiply_add_fusion), kind=kOutput, calls=%fused_computation | convolution fusion | flops 539099136 | bytes 4196352 | tf_op jit(solution)/shard_map/dot_general | solution.py:66
  39.5 16.2 %all-to-all-done.1 = bf16[16,32,2048]{2,1,0:T(8,128)(2,1)} async-done(((bf16[16,32,2048]{2,1,0:T(8,128)(2,1)}), bf16[16,32,2048]{2,1,0:T(8,128)(2,1)}, u32[]{:S(2)}, u32[]{:S(2)}) %all-to-all-start.1) | async-done | bytes 2097184 | tf_op jit(solution)/shard_map/all_to_all | solution.py:69
  55.7 7.8 %all-to-all-start.3 = ((bf16[16,32,2048]{2,1,0:T(8,128)(2,1)}), bf16[16,32,2048]{2,1,0:T(8,128)(2,1)}, u32[]{:S(2)}, u32[]{:S(2)}) async-start(bf16[16,32,2048]{2,1,0:T(8,128)(2,1)} %bitcast.81), calls=%async_computation.3 | async-start | bytes 4194304 | tf_op jit(solution)/shard_map/all_to_all | solution.py:72
  63.7 3.5 %fusion.6 = f32[512,512]{1,0:T(8,128)S(1)} fusion(bf16[512,2048]{1,0:T(8,128)(2,1)} %bitcast.8, bf16[1,2048,512]{2,1,0:T(8,128)(2,1)} %param.10), kind=kOutput, calls=%fused_computation.12 | convolution fusion | flops 1073741824 | bytes 5242880 | tf_op jit(solution)/shard_map/dot_general | solution.py:21
  67.2 1.0 copy-done.4
  68.2 2.6 %convolution_convert_fusion.5 = bf16[512,2048]{1,0:T(8,128)(2,1)} fusion(bf16[1,512,2048]{2,1,0:T(8,128)(2,1)S(1)} %copy-done, f32[512,512]{1,0:T(8,128)S(1)} %fusion.6, pred[512]{0:T(512)(128)(4,1)S(1)} %lt.37), kind=kOutput, calls=%fused_computation.5 | convolution fusion | flops 1076363264 | bytes 5243392 | tf_op jit(solution)/shard_map/dot_general | solution.py:25
  70.8 18.6 %all-to-all-done.3 = bf16[16,32,2048]{2,1,0:T(8,128)(2,1)} async-done(((bf16[16,32,2048]{2,1,0:T(8,128)(2,1)}), bf16[16,32,2048]{2,1,0:T(8,128)(2,1)}, u32[]{:S(2)}, u32[]{:S(2)}) %all-to-all-start.3) | async-done | bytes 2097184 | tf_op jit(solution)/shard_map/all_to_all | solution.py:72
  89.4 3.5 %fusion.14 = bf16[512,512]{1,0:T(8,128)(2,1)S(1)} fusion(bf16[512,2048]{1,0:T(8,128)(2,1)} %bitcast.15, bf16[1,512,2048]{2,1,0:T(8,128)(2,1)S(1)} %copy-done, f32[512,512]{1,0:T(8,128)} %copy-done.4, pred[512]{0:T(512)(128)(4,1)S(1)} %lt.37), kind=kOutput, calls=%fused_computation.17 | convolution fusion | flops 1076363264 | bytes 5767680 | tf_op jit(solution)/shard_map/dot_general | solution.py:26
  92.9 2.7 %convolution_convert_fusion.4 = bf16[512,2048]{1,0:T(8,128)(2,1)} fusion(bf16[512,512]{1,0:T(8,128)(2,1)S(1)} %fusion.14, bf16[1,2048,512]{2,1,0:T(8,128)(2,1)S(1)} %copy-done.3), kind=kOutput, calls=%fused_computation.4 | convolution fusion | flops 1074790400 | bytes 4718592 | tf_op jit(solution)/shard_map/dot_general | solution.py:40
  95.6 4.7 %fusion.1 = bf16[1,512,2048]{2,1,0:T(8,128)(2,1)} fusion(bf16[512,2048]{1,0:T(8,128)(2,1)} %bitcast.15, f32[512,512]{1,0:T(8,128)} %copy-done.4, pred[512]{0:T(512)(128)(4,1)S(1)} %lt.37), kind=kOutput, calls=%fused_computation.7 | convolution fusion | flops 1076363264 | bytes 5243392 | tf_op jit(solution)/shard_map/dot_general | solution.py:31
  100.3 119.4 %all-reduce.3.cloned.1.call-done = (bf16[512,2048]{1,0:T(8,128)(2,1)}, bf16[512,2048]{1,0:T(8,128)(2,1)}) async-done(((bf16[512,2048]{1,0:T(8,128)(2,1)}, bf16[512,2048]{1,0:T(8,128)(2,1)}), (bf16[512,2048]{1,0:T(8,128)(2,1)}, bf16[512,2048]{1,0:T(8,128)(2,1)})) %all-reduce.3.cloned.1.call-update) | async-done | bytes 4194320 | tf_op jit(solution)/shard_map/psum | solution.py:92
  219.7 1.6 convert_convert_fusion.1
  221.2 7.3 %all-to-all-start.2 = ((bf16[16,32,128]{2,1,0:T(8,128)(2,1)}), bf16[16,32,128]{2,1,0:T(8,128)(2,1)S(1)}, u32[]{:S(2)}, u32[]{:S(2)}) async-start(bf16[16,32,128]{2,1,0:T(8,128)(2,1)} %bitcast.11), calls=%async_computation.2 | async-start | bytes 262144 | tf_op jit(solution)/shard_map/all_to_all | solution.py:99
  228.5 4.2 %fusion = bf16[1,2048,512]{2,1,0:T(8,128)(2,1)} fusion(bf16[512,2048]{1,0:T(8,128)(2,1)} %bitcast.8, bf16[512,512]{1,0:T(8,128)(2,1)S(1)} %fusion.14), kind=kOutput, calls=%fused_computation.6 | convolution fusion | flops 1074790400 | bytes 4718592 | tf_op jit(solution)/shard_map/dot_general | solution.py:34
  232.7 1.5 convert_convert_fusion
  234.3 0.9 all-to-all-done.2
  235.1 6.4 %all-to-all-start.4 = ((bf16[16,32,128]{2,1,0:T(8,128)(2,1)}), bf16[16,32,128]{2,1,0:T(8,128)(2,1)S(1)}, u32[]{:S(2)}, u32[]{:S(2)}) async-start(bf16[16,32,128]{2,1,0:T(8,128)(2,1)} %bitcast.16), calls=%async_computation.4 | async-start | bytes 262144 | tf_op jit(solution)/shard_map/all_to_all | solution.py:106
  241.5 0.9 fusion.17
  242.4 5.7 %all-to-all-done.4 = bf16[16,32,128]{2,1,0:T(8,128)(2,1)S(1)} async-done(((bf16[16,32,128]{2,1,0:T(8,128)(2,1)}), bf16[16,32,128]{2,1,0:T(8,128)(2,1)S(1)}, u32[]{:S(2)}, u32[]{:S(2)}) %all-to-all-start.4) | async-done | bytes 131104 | tf_op jit(solution)/shard_map/all_to_all | solution.py:106
  248.1 0.9 convolution_reduce_fusion
  (28 shorter events, 1.2 us)
Async XLA Ops:
  7.2 61.0 %copy-start = (bf16[1,512,2048]{2,1,0:T(8,128)(2,1)S(1)}, bf16[1,512,2048]{2,1,0:T(8,128)(2,1)}, u32[]{:S(2)}) copy-start(bf16[1,512,2048]{2,1,0:T(8,128)(2,1)} %param.11) | copy-start | bytes 6291460
  10.1 13.6 %all-to-all-start = ((bf16[16,1,2]{2,1,0:T(2,128)(2,1)}), bf16[16,1,2]{2,1,0:T(2,128)(2,1)S(1)}, u32[]{:S(2)}, u32[]{:S(2)}) async-start(bf16[16,1,2]{2,1,0:T(2,128)(2,1)} %copy.41), calls=%async_computation | async-start | bytes 16384 | tf_op jit(solution)/shard_map/all_to_all | solution.py:79
  23.7 5.8 %copy-start.2 = (f32[128,2]{0,1:T(2,128)S(1)}, f32[128,2]{0,1:T(2,128)}, u32[]{:S(2)}) copy-start(f32[128,2]{0,1:T(2,128)} %param.8) | copy-start | bytes 3076
  23.7 6.0 %copy-start.1 = (bf16[128,2048]{1,0:T(8,128)(2,1)S(1)}, bf16[128,2048]{1,0:T(8,128)(2,1)}, u32[]{:S(2)}) copy-start(bf16[128,2048]{1,0:T(8,128)(2,1)} %param.9) | copy-start | bytes 1572868
  23.7 31.9 %all-to-all-start.1 = ((bf16[16,32,2048]{2,1,0:T(8,128)(2,1)}), bf16[16,32,2048]{2,1,0:T(8,128)(2,1)}, u32[]{:S(2)}, u32[]{:S(2)}) async-start(bf16[16,32,2048]{2,1,0:T(8,128)(2,1)} %bitcast.82), calls=%async_computation.1 | async-start | bytes 4194304 | tf_op jit(solution)/shard_map/all_to_all | solution.py:69
  55.7 33.7 %all-to-all-start.3 = ((bf16[16,32,2048]{2,1,0:T(8,128)(2,1)}), bf16[16,32,2048]{2,1,0:T(8,128)(2,1)}, u32[]{:S(2)}, u32[]{:S(2)}) async-start(bf16[16,32,2048]{2,1,0:T(8,128)(2,1)} %bitcast.81), calls=%async_computation.3 | async-start | bytes 4194304 | tf_op jit(solution)/shard_map/all_to_all | solution.py:72
  63.4 156.3 %all-reduce.3.cloned.1.call-start = ((), (), s32[]{:S(2)}) async-start(), calls=%async_computation.5 | async-start | bytes 8388608 | tf_op jit(solution)/shard_map/psum | solution.py:92
  67.2 1.0 copy-start.4
  89.4 3.5 %copy-start.3 = (bf16[1,2048,512]{2,1,0:T(8,128)(2,1)S(1)}, bf16[1,2048,512]{2,1,0:T(8,128)(2,1)}, u32[]{:S(2)}) copy-start(bf16[1,2048,512]{2,1,0:T(8,128)(2,1)} %param.10) | copy-start | bytes 6291460
  221.2 13.9 %all-to-all-start.2 = ((bf16[16,32,128]{2,1,0:T(8,128)(2,1)}), bf16[16,32,128]{2,1,0:T(8,128)(2,1)S(1)}, u32[]{:S(2)}, u32[]{:S(2)}) async-start(bf16[16,32,128]{2,1,0:T(8,128)(2,1)} %bitcast.11), calls=%async_computation.2 | async-start | bytes 262144 | tf_op jit(solution)/shard_map/all_to_all | solution.py:99
  235.1 13.0 %all-to-all-start.4 = ((bf16[16,32,128]{2,1,0:T(8,128)(2,1)}), bf16[16,32,128]{2,1,0:T(8,128)(2,1)S(1)}, u32[]{:S(2)}, u32[]{:S(2)}) async-start(bf16[16,32,128]{2,1,0:T(8,128)(2,1)} %bitcast.16), calls=%async_computation.4 | async-start | bytes 262144 | tf_op jit(solution)/shard_map/all_to_all | solution.py:106
Sparse Core Ops, SparseCore 0:
  95.7 123.8 all-reduce.2
where the time goes:
time: 257 us; the launch traced here: 256 us
  waiting for transfers between devices  163 us (63%)
  starting transfers between devices  34.7 us (14%)
  matrix products  29.7 us (12%)
  between operations  14.1 us (5%)
  local copies, waits for them, and re-layouts  9.78 us (4%)
  other arithmetic  4.77 us (2%)
    psum x1, waiting for transfers between devices, local(): lax.psum(out_part.astype(jnp.bfloat16), 'rep').astype(jnp.float32)  119 us
    all_to_all x1, waiting for transfers between devices, local(): lax.all_to_all(sent_grad.reshape(n_exp, capacity, width), 'exp', split_ax...  18.6 us
    all_to_all x1, waiting for transfers between devices, local(): lax.all_to_all(sent_in.reshape(n_exp, capacity, width), 'exp', split_axis...  16.2 us
    all_to_all x1, starting transfers between devices, local(): lax.all_to_all(sent_grad.reshape(n_exp, capacity, width), 'exp', split_ax...  7.76 us
    all_to_all x1, starting transfers between devices, local(): lax.all_to_all(count_parts, 'exp', split_axis=0, concat_axis=0, tiled=True)  7.48 us
    all_to_all x1, starting transfers between devices, local(): lax.all_to_all(summed_out.astype(jnp.bfloat16).reshape(n_exp, capacity, c...  7.27 us
    all_to_all x1, starting transfers between devices, local(): lax.all_to_all(summed_dx.astype(jnp.bfloat16).reshape(n_exp, capacity, co...  6.37 us
    mul x3, local copies, waits for them, and re-layouts, local(): gate_values[:, :, None] * grad_out[:, None, :].astype(jnp.float32)  6.2 us
  transfers between devices with their start and end apart: 6, of which 6 were waited for; matrix products, arithmetic and copies ran while one was open for 12% of the time, Pallas kernels for 0%

commit v1 on v0

--- a/solution.py
+++ b/solution.py
@@ -89,7 +89,7 @@
         rows_in, rows_grad, live_mask, up_weight, down_weight
     )
     total_out, total_dx = (
-        lax.psum(out_part.astype(jnp.bfloat16), "rep").astype(jnp.float32),
+        jnp.sum(lax.all_gather(out_part.astype(jnp.bfloat16), "rep"), axis=0).astype(jnp.float32),
         lax.psum(dx_part.astype(jnp.bfloat16), "rep").astype(jnp.float32),
     )
     col_start = lax.axis_index("rep") * cols

time: 257 us -> 428 us (1.67)
  waiting for transfers between devices: 163 us -> 317 us
  other arithmetic: 4.77 us -> 17.8 us
    all_gather x0 -> x1, waiting for transfers between devices: none -> 163 us  [local(): lax.all_gather(out_part.astype(jnp.bfloat16), 'rep')]
    reduce_sum x0 -> x1, other arithmetic: none -> 13 us  [local(): jnp.sum(lax.all_gather(out_part.astype(jnp.bfloat16), 'rep'), axis=0)]
    psum x1, waiting for transfers between devices: 119 us -> 108 us  [local(): lax.psum(dx_part.astype(jnp.bfloat16), 'rep').astype(jnp.float32)]
    all_to_all x1, waiting for transfers between devices: 5.73 us -> 0.01 us  [local(): lax.all_to_all(summed_dx.astype(jnp.bfloat16).reshape(n_exp, capacity, co...]
    all_to_all x1, waiting for transfers between devices: 0.86 us -> 5.73 us  [local(): lax.all_to_all(summed_out.astype(jnp.bfloat16).reshape(n_exp, capacity, c...]
  transfers between devices with their start and end apart: 6 -> 7, of which waited for: 6 -> 6; matrix products, arithmetic and copies ran while one was open for 12% -> 11% of each run, Pallas kernels for 0% -> 0%
where the time goes in v1:
time: 428 us; the launch traced here: 426 us
  waiting for transfers between devices  317 us (74%)
  starting transfers between devices  35.6 us (8%)
  matrix products  32.5 us (8%)
  other arithmetic  17.8 us (4%)
  between operations  14.1 us (3%)
  local copies, waits for them, and re-layouts  8.84 us (2%)
    all_gather x1, waiting for transfers between devices, local(): lax.all_gather(out_part.astype(jnp.bfloat16), 'rep')  163 us
    psum x1, waiting for transfers between devices, local(): lax.psum(dx_part.astype(jnp.bfloat16), 'rep').astype(jnp.float32)  108 us
    all_to_all x1, waiting for transfers between devices, local(): lax.all_to_all(sent_grad.reshape(n_exp, capacity, width), 'exp', split_ax...  21.8 us
    all_to_all x1, waiting for transfers between devices, local(): lax.all_to_all(sent_in.reshape(n_exp, capacity, width), 'exp', split_axis...  16.1 us
    reduce_sum x1, other arithmetic, local(): jnp.sum(lax.all_gather(out_part.astype(jnp.bfloat16), 'rep'), axis=0)  13 us
  transfers between devices with their start and end apart: 7, of which 6 were waited for; matrix products, arithmetic and copies ran while one was open for 11% of the time, Pallas kernels for 0%

profile of v1, /device:TPU:2, one launch (start us, length us, event | category | flops | bytes accessed | tf_op | source)
XLA Modules:
  0.0 426.2 jit_solution(2291011378235778560)
XLA Ops:
  7.2 0.9 copy.37
  8.4 0.6 reduce-window.6
  9.0 0.2 slice_reduce_fusion
  9.2 0.1 convert_reduce_fusion
  9.4 0.7 copy.41
  10.1 7.5 %all-to-all-start = ((bf16[16,1,2]{2,1,0:T(2,128)(2,1)}), bf16[16,1,2]{2,1,0:T(2,128)(2,1)S(1)}, u32[]{:S(2)}, u32[]{:S(2)}) async-start(bf16[16,1,2]{2,1,0:T(2,128)(2,1)} %copy.41), calls=%async_computation | async-start | bytes 16384 | tf_op jit(solution)/shard_map/all_to_all | solution.py:79
  17.8 0.7 multiply_add_fusion.1
  18.6 3.1 convolution_convert_fusion.1
  21.6 2.1 all-to-all-done
  23.7 5.8 %all-to-all-start.1 = ((bf16[16,32,2048]{2,1,0:T(8,128)(2,1)}), bf16[16,32,2048]{2,1,0:T(8,128)(2,1)}, u32[]{:S(2)}, u32[]{:S(2)}) async-start(bf16[16,32,2048]{2,1,0:T(8,128)(2,1)} %bitcast.83), calls=%async_computation.1 | async-start | bytes 4194304 | tf_op jit(solution)/shard_map/all_to_all | solution.py:69
  29.5 2.4 mul.76
  31.9 3.7 mul.77
  35.9 3.7 convolution_convert_fusion
  39.6 16.1 %all-to-all-done.1 = bf16[16,32,2048]{2,1,0:T(8,128)(2,1)} async-done(((bf16[16,32,2048]{2,1,0:T(8,128)(2,1)}), bf16[16,32,2048]{2,1,0:T(8,128)(2,1)}, u32[]{:S(2)}, u32[]{:S(2)}) %all-to-all-start.1) | async-done | bytes 2097184 | tf_op jit(solution)/shard_map/all_to_all | solution.py:69
  55.7 7.7 %all-to-all-start.3 = ((bf16[16,32,2048]{2,1,0:T(8,128)(2,1)}), bf16[16,32,2048]{2,1,0:T(8,128)(2,1)}, u32[]{:S(2)}, u32[]{:S(2)}) async-start(bf16[16,32,2048]{2,1,0:T(8,128)(2,1)} %bitcast.84), calls=%async_computation.3 | async-start | bytes 4194304 | tf_op jit(solution)/shard_map/all_to_all | solution.py:72
  63.7 3.8 fusion.6
  67.5 21.8 %all-to-all-done.3 = bf16[16,32,2048]{2,1,0:T(8,128)(2,1)} async-done(((bf16[16,32,2048]{2,1,0:T(8,128)(2,1)}), bf16[16,32,2048]{2,1,0:T(8,128)(2,1)}, u32[]{:S(2)}, u32[]{:S(2)}) %all-to-all-start.3) | async-done | bytes 2097184 | tf_op jit(solution)/shard_map/all_to_all | solution.py:72
  89.4 4.0 fusion.14
  93.4 2.7 convolution_convert_fusion.4
  96.1 4.6 %convolution_convert_fusion.5 = bf16[512,2048]{1,0:T(8,128)(2,1)} fusion(bf16[1,512,2048]{2,1,0:T(8,128)(2,1)} %param.11, f32[512,512]{1,0:T(8,128)} %fusion.6, pred[512]{0:T(512)(128)(4,1)S(1)} %lt.37), kind=kOutput, calls=%fused_computation.5 | convolution fusion | flops 1076363264 | bytes 5243392 | tf_op jit(solution)/shard_map/dot_general | solution.py:25
  100.7 4.7 %fusion.1 = bf16[1,512,2048]{2,1,0:T(8,128)(2,1)} fusion(bf16[512,2048]{1,0:T(8,128)(2,1)} %bitcast.16, f32[512,512]{1,0:T(8,128)} %fusion.6, pred[512]{0:T(512)(128)(4,1)S(1)} %lt.37), kind=kOutput, calls=%fused_computation.7 | convolution fusion | flops 1076363264 | bytes 5243392 | tf_op jit(solution)/shard_map/dot_general | solution.py:31
  105.4 108.2 %all-reduce.2.cloned.1.call-done = bf16[512,2048]{1,0:T(8,128)(2,1)} async-done(((bf16[512,2048]{1,0:T(8,128)(2,1)}), bf16[512,2048]{1,0:T(8,128)(2,1)}) %all-reduce.2.cloned.1.call-update) | async-done | bytes 2097168 | tf_op jit(solution)/shard_map/psum | solution.py:93
  213.6 1.5 convert_convert_fusion
  215.1 7.3 %all-to-all-start.4 = ((bf16[16,32,128]{2,1,0:T(8,128)(2,1)}), bf16[16,32,128]{2,1,0:T(8,128)(2,1)S(1)}, u32[]{:S(2)}, u32[]{:S(2)}) async-start(bf16[16,32,128]{2,1,0:T(8,128)(2,1)} %bitcast.17), calls=%async_computation.4 | async-start | bytes 262144 | tf_op jit(solution)/shard_map/all_to_all | solution.py:106
  222.4 4.2 fusion
  226.6 163.3 %all-gather.3.cloned.1.call-done = bf16[8192,2048]{1,0:T(8,128)(2,1)} async-done(((bf16[512,2048]{1,0:T(8,128)(2,1)}), bf16[8192,2048]{1,0:T(8,128)(2,1)}) %all-gather.3.cloned.1.call-update) | async-done | bytes 33554448 | tf_op jit(solution)/shard_map/all_gather | solution.py:92
  390.0 13.0 %reduce_sum.69 = bf16[512,2048]{1,0:T(8,128)(2,1)} reduce(bf16[16,512,2048]{2,1,0:T(8,128)(2,1)} %bitcast.82, bf16[]{:T(256)} %constant.46.clone.1), dimensions={0}, to_apply=%region_5.6 | reduce | flops 15728640 | bytes 35651584 | tf_op jit(solution)/shard_map/reduce_sum | solution.py:92
  403.0 1.5 convert_convert_fusion.1
  404.6 7.3 %all-to-all-start.2 = ((bf16[16,32,128]{2,1,0:T(8,128)(2,1)}), bf16[16,32,128]{2,1,0:T(8,128)(2,1)S(1)}, u32[]{:S(2)}, u32[]{:S(2)}) async-start(bf16[16,32,128]{2,1,0:T(8,128)(2,1)} %bitcast.12), calls=%async_computation.2 | async-start | bytes 262144 | tf_op jit(solution)/shard_map/all_to_all | solution.py:99
  411.9 0.9 convolution_reduce_fusion
  412.8 5.7 %all-to-all-done.2 = bf16[16,32,128]{2,1,0:T(8,128)(2,1)S(1)} async-done(((bf16[16,32,128]{2,1,0:T(8,128)(2,1)}), bf16[16,32,128]{2,1,0:T(8,128)(2,1)S(1)}, u32[]{:S(2)}, u32[]{:S(2)}) %all-to-all-start.2) | async-done | bytes 131104 | tf_op jit(solution)/shard_map/all_to_all | solution.py:99
  418.5 0.9 fusion.17
  (28 shorter events, 1.3 us)
Async XLA Ops:
  7.2 56.6 %copy-start = (bf16[1,2048,512]{2,1,0:T(8,128)(2,1)S(1)}, bf16[1,2048,512]{2,1,0:T(8,128)(2,1)}, u32[]{:S(2)}) copy-start(bf16[1,2048,512]{2,1,0:T(8,128)(2,1)} %param.10) | copy-start | bytes 6291460
  10.1 13.6 %all-to-all-start = ((bf16[16,1,2]{2,1,0:T(2,128)(2,1)}), bf16[16,1,2]{2,1,0:T(2,128)(2,1)S(1)}, u32[]{:S(2)}, u32[]{:S(2)}) async-start(bf16[16,1,2]{2,1,0:T(2,128)(2,1)} %copy.41), calls=%async_computation | async-start | bytes 16384 | tf_op jit(solution)/shard_map/all_to_all | solution.py:79
  23.7 5.8 %copy-start.1 = (bf16[128,2048]{1,0:T(8,128)(2,1)S(1)}, bf16[128,2048]{1,0:T(8,128)(2,1)}, u32[]{:S(2)}) copy-start(bf16[128,2048]{1,0:T(8,128)(2,1)} %param.9) | copy-start | bytes 1572868
  23.7 31.9 %all-to-all-start.1 = ((bf16[16,32,2048]{2,1,0:T(8,128)(2,1)}), bf16[16,32,2048]{2,1,0:T(8,128)(2,1)}, u32[]{:S(2)}, u32[]{:S(2)}) async-start(bf16[16,32,2048]{2,1,0:T(8,128)(2,1)} %bitcast.83), calls=%async_computation.1 | async-start | bytes 4194304 | tf_op jit(solution)/shard_map/all_to_all | solution.py:69
  31.9 3.7 copy-start.2
  55.7 33.7 %all-to-all-start.3 = ((bf16[16,32,2048]{2,1,0:T(8,128)(2,1)}), bf16[16,32,2048]{2,1,0:T(8,128)(2,1)}, u32[]{:S(2)}, u32[]{:S(2)}) async-start(bf16[16,32,2048]{2,1,0:T(8,128)(2,1)} %bitcast.84), calls=%async_computation.3 | async-start | bytes 4194304 | tf_op jit(solution)/shard_map/all_to_all | solution.py:72
  63.4 150.2 %all-reduce.2.cloned.1.call-start = ((), (), s32[]{:S(2)}) async-start(), calls=%async_computation.5 | async-start | bytes 4194304 | tf_op jit(solution)/shard_map/psum | solution.py:93
  96.1 293.9 %all-gather.3.cloned.1.call-start = ((), (), s32[]{:S(2)}) async-start(), calls=%async_computation.6 | async-start | bytes 35651584 | tf_op jit(solution)/shard_map/all_gather | solution.py:92
  215.1 189.4 %all-to-all-start.4 = ((bf16[16,32,128]{2,1,0:T(8,128)(2,1)}), bf16[16,32,128]{2,1,0:T(8,128)(2,1)S(1)}, u32[]{:S(2)}, u32[]{:S(2)}) async-start(bf16[16,32,128]{2,1,0:T(8,128)(2,1)} %bitcast.17), calls=%async_computation.4 | async-start | bytes 262144 | tf_op jit(solution)/shard_map/all_to_all | solution.py:106
  404.6 13.9 %all-to-all-start.2 = ((bf16[16,32,128]{2,1,0:T(8,128)(2,1)}), bf16[16,32,128]{2,1,0:T(8,128)(2,1)S(1)}, u32[]{:S(2)}, u32[]{:S(2)}) async-start(bf16[16,32,128]{2,1,0:T(8,128)(2,1)} %bitcast.12), calls=%async_computation.2 | async-start | bytes 262144 | tf_op jit(solution)/shard_map/all_to_all | solution.py:99
Sparse Core Ops, SparseCore 0:
  96.2 117.3 all-reduce.1
  215.4 174.5 all-gather.2
